TPU v7x, 256 devices: a whole 4x4x8 slice. The times are simulated.
256 devices in a mesh: shot: 16 (over y_lo, z), gx: 16 (over y_hi, x, core).
Axes of the slice: x: 4, y: 4 (y_hi: 2, y_lo: 2; y = y_hi * 2 + y_lo), z: 8, core: 2. Of those that a mesh axis runs over, the one named last changes fastest.
Arguments:
- source_prev: float32 [16, 256, 64, 128], P('shot', 'gx'), may hold values from -6 to 6
- source_now: float32 [16, 256, 64, 128], P('shot', 'gx'), may hold values from -6 to 6
- receiver_prev: float32 [16, 256, 64, 128], P('shot', 'gx'), may hold values from -6 to 6
- receiver_now: float32 [16, 256, 64, 128], P('shot', 'gx'), may hold values from -6 to 6
- courant: float32 [256, 64, 128], P('gx'), may hold values from 0.05 to 0.3
- source_cells: int32 [16, 8], P('shot'), may hold values from 0 to 2097151
- wavelet: float32 [16, 2, 8], P('shot'), may hold values from -128 to 128
- receiver_cells: int32 [16, 512], P('shot'), may hold values from 0 to 2097151
- receiver_data: float32 [16, 2, 512], P('shot'), may hold values from -128 to 128
- offsets: int32 [9], replicated, may hold values from -8 to 8, as said below
- conv_weight: float32 [64, 9, 3, 3, 3], replicated, may hold values from -1.25 to 1.25
- conv_bias: float32 [64], replicated, may hold values from -3 to 3
Outputs:
- summary: float32 [64, 64, 512], P(None, 'gx', 'shot')
Inputs may be any that keep to these rules, and one draw needn't show every extreme that they name: The offsets are distinct and include -8 and 8.
All inputs are finite; a program needn't handle non-finite values.
Results may differ from a plain program's by a relative error of at most 0.0003.
Values sent between devices are 32-bit elements; how exact they have to be, the bound alone decides.
No kernel may reach another device: no remote copies, remote signals or barrier semaphores. Data moves between devices by JAX's collectives and lax.ppermute only.
A program may use at most 64 MiB of HBM per device.

v0:
```python
import jax
import jax.numpy as jnp
from jax import lax
from jax.sharding import PartitionSpec as P

HMAX = 8


def padded_2(block, sides, width):
    for axis, dim in sides:
        count = lax.axis_size(axis)
        forward = [(i, i + 1) for i in range(count - 1)]
        backward = [(target, source) for source, target in forward]
        low = lax.ppermute(
            lax.slice_in_dim(block, block.shape[dim] - width, None, axis=dim), axis, forward
        )
        high = lax.ppermute(lax.slice_in_dim(block, 0, width, axis=dim), axis, backward)
        block = jnp.concatenate([low, block, high], axis=dim)
    return block


def inject(cells_here, first_x, cell_index, amplitudes, size_y, size_z):
    plane_size = size_y * size_z
    column = cell_index // plane_size
    within = cell_index % plane_size
    local_x = column - first_x
    inside = (local_x >= 0) & (local_x < cells_here)
    target = jnp.where(inside, local_x * plane_size + within, cells_here * plane_size)
    flat_cells = jnp.zeros((cells_here * plane_size + 1,), jnp.float32).at[target].add(amplitudes)
    return flat_cells[:-1].reshape(cells_here, size_y, size_z)


def laplace_step(previous, extended, courant, sources):
    center = extended[:, 1:-1]
    padded = jnp.pad(center, ((0, 0), (0, 0), (1, 1), (1, 1)))
    laplace = extended[:, 2:] + extended[:, :-2]
    laplace = laplace + padded[:, :, 2:, 1:-1] + padded[:, :, :-2, 1:-1]
    laplace = laplace + padded[:, :, 1:-1, 2:] + padded[:, :, 1:-1, :-2] - 6.0 * center
    return 2.0 * center - previous + courant * laplace + sources


def coarsen(image_block):
    size_x, size_y, size_z = image_block.shape
    return image_block.reshape(size_x // 4, 4, size_y // 4, 4, size_z // 4, 4).mean(axis=(1, 3, 5))


def offset_image(wide, offsets, margin, cells_x):

    def per_offset(offset_value):
        forward_part = lax.dynamic_slice_in_dim(wide, margin + offset_value, cells_x, 1)
        backward_part = lax.dynamic_slice_in_dim(wide, margin - offset_value, cells_x, 1)
        image_block = forward_part[0] * backward_part[1] + forward_part[2] * backward_part[3]
        return coarsen(image_block)

    return lax.map(per_offset, offsets)


def conv_apply(padded, conv_weight, conv_bias):
    channels, span_x, span_y, span_z = padded.shape
    size_x, size_y, size_z = (span_x - 2, span_y - 2, span_z - 2)
    patches = jnp.stack(
        [
            padded[:, step_x : step_x + size_x, step_y : step_y + size_y, step_z : step_z + size_z]
            for step_x in range(3)
            for step_y in range(3)
            for step_z in range(3)
        ],
        axis=1,
    )
    patches = patches.reshape(channels * 27, size_x * size_y * size_z)
    matrix = conv_weight.reshape(conv_weight.shape[0], channels * 27)
    result = jnp.dot(
        matrix, patches, precision=lax.Precision.HIGHEST, preferred_element_type=jnp.float32
    )
    result = result + conv_bias[:, None]
    return result.reshape(conv_weight.shape[0], size_x, size_y * size_z)


def local(
    source_prev,
    source_now,
    receiver_prev,
    receiver_now,
    courant,
    source_cells,
    wavelet,
    receiver_cells,
    receiver_data,
    offsets,
    conv_weight,
    conv_bias,
):
    cells_x, size_y, size_z = courant.shape
    slab_index = lax.axis_index("gx")
    previous = jnp.stack([source_prev[0], receiver_prev[0]])
    current = jnp.stack([source_now[0], receiver_now[0]])
    levels = []
    for step_index in range(2):
        extended = padded_2(current, (("gx", 1),), 1)
        first_x = slab_index * cells_x
        advanced = laplace_step(
            previous,
            extended,
            courant,
            jnp.stack(
                [
                    inject(
                        cells_x, first_x, source_cells[0], wavelet[0, step_index], size_y, size_z
                    ),
                    inject(
                        cells_x,
                        first_x,
                        receiver_cells[0],
                        receiver_data[0, step_index],
                        size_y,
                        size_z,
                    ),
                ]
            ),
        )
        previous, current = (current, advanced)
        levels.append(advanced)
    fields = jnp.concatenate(levels, axis=0)
    wide = padded_2(fields, (("gx", 1),), HMAX)
    coarse = offset_image(wide, offsets, HMAX, cells_x)
    summed = lax.psum(coarse, "shot")
    rimmed = padded_2(summed, (("gx", 1),), 1)
    row_count = summed.shape[2] // lax.axis_size("shot")
    padded = jnp.pad(rimmed, ((0, 0), (0, 0), (1, 1), (1, 1)))
    window = lax.dynamic_slice_in_dim(padded, lax.axis_index("shot") * row_count, row_count + 2, 2)
    return conv_apply(window, conv_weight, conv_bias)


def solution(mesh):
    in_specs = (
        P("shot", "gx", None, None),
        P("shot", "gx", None, None),
        P("shot", "gx", None, None),
        P("shot", "gx", None, None),
        P("gx", None, None),
        P("shot", None),
        P("shot", None, None),
        P("shot", None),
        P("shot", None, None),
        P(),
        P(),
        P(),
    )
    out_specs = P(None, "gx", "shot")
    return jax.shard_map(local, mesh=mesh, in_specs=in_specs, out_specs=out_specs, check_vma=False)
```

profile of v0, /device:TPU:7, one launch (start us, length us, event | category | flops | bytes accessed | tf_op | source)
XLA Modules:
  0.0 510.2 jit_solution(17402110244412481747)
XLA Ops:
  6.5 1.1 constant_dynamic-update-slice_fusion.1
  8.8 2.6 collective-permute-start
  11.4 6.6 %collective-permute-start.1 = (f32[2,1,64,128]{3,2,1,0:T(8,128)S(1)}, f32[2,1,64,128]{3,2,1,0:T(8,128)S(1)}, u32[]{:S(2)}, u32[]{:S(2)}) collective-permute-start(f32[2,1,64,128]{3,2,1,0:T(8,128)S(1)} %get-tuple-element.86), channel_id=1, source_target_pairs={{0,1},{1,2},{2,3},{3,4},{4,5},{5,6},{6,7},{7,8},{8,9},{9,10},{10,1... | collective-permute-start | bytes 196616 | tf_op jit(solution)/shard_map/ppermute | solution.py:14
  20.9 4.0 scatter_custom_fusion.1
  25.8 1.9 fusion.10
  27.7 1.9 collective-permute-start.2
  29.7 7.3 %collective-permute-start.3 = (f32[2,1,64,128]{3,2,1,0:T(8,128)S(1)}, f32[2,1,64,128]{3,2,1,0:T(8,128)S(1)}, u32[]{:S(2)}, u32[]{:S(2)}) collective-permute-start(f32[2,1,64,128]{3,2,1,0:T(8,128)S(1)} %get-tuple-element.84), channel_id=1, source_target_pairs={{0,1},{1,2},{2,3},{3,4},{4,5},{5,6},{6,7},{7,8},{8,9},{9,10},{10,1... | collective-permute-start | bytes 196616 | tf_op jit(solution)/shard_map/ppermute | solution.py:14
  36.9 4.0 scatter_custom_fusion.3
  42.6 1.9 fusion.18
  44.5 1.2 fusion.2
  45.7 3.5 collective-permute-start.4
  49.2 1.9 collective-permute-start.5
  51.2 10.1 %collective-permute-done.4 = f32[4,8,64,128]{3,2,1,0:T(8,128)} collective-permute-done((f32[4,8,64,128]{3,2,1,0:T(8,128)}, f32[4,8,64,128]{3,2,1,0:T(8,128)}, u32[]{:S(2)}, u32[]{:S(2)}) %collective-permute-start.4) | collective-permute-done | bytes 1048608 | tf_op jit(solution)/shard_map/ppermute | solution.py:14
  61.3 7.8 %collective-permute-done.5 = f32[4,8,64,128]{3,2,1,0:T(8,128)} collective-permute-done((f32[4,8,64,128]{3,2,1,0:T(8,128)S(1)}, f32[4,8,64,128]{3,2,1,0:T(8,128)}, u32[]{:S(2)}, u32[]{:S(2)}) %collective-permute-start.5) | collective-permute-done | bytes 1048608 | tf_op jit(solution)/shard_map/ppermute | solution.py:17
  69.1 4.0 pad_maximum_fusion
  73.1 277.4 %while.13 = (s32[]{:T(128)}, f32[9,4,16,32]{3,2,1,0:T(8,128)}, s32[9]{0:T(128)S(1)}, f32[4,32,64,128]{3,2,1,0:T(8,128)}, s32[]{:T(128)}, /*index=5*/s32[]{:T(128...) while((s32[]{:T(128)}, f32[9,4,16,32]{3,2,1,0:T(8,128)}, s32[9]{0:T(128)S(1)}, ...), condition=%wide.region_6.7_spmd, body=%wide.region_4.6_spmd.sunk | while | flops 524301 | bytes 4244249 | solution.py:55
  75.9 1.7 fusion.56
  77.6 18.6 %add.415 = f32[4,4,16,4,32,4]{5,4,3,2,1,0:T(8,128)} reshape(f32[1,16,64,128]{3,2,1,0:T(8,128)S(1)} %fusion.56) | data formatting | bytes 1048576 | tf_op jit(solution)/shard_map/while/body/eval_jaxpr/add | solution.py:52
  96.2 7.1 %reduce_sum.14 = f32[4,16,32]{2,1,0:T(8,128)S(1)} reduce(f32[4,4,16,4,32,4]{5,4,3,2,1,0:T(8,128)} %add.415, f32[]{:T(128)} %constant.122.clone.1..sunk), dimensions={1,3,5}, to_apply=%region_5.5 | reduce | flops 129024 | bytes 532484 | tf_op jit(solution)/shard_map/while/body/eval_jaxpr/reduce_sum | solution.py:44
  106.7 1.7 fusion.56
  108.4 18.6 %add.415 = f32[4,4,16,4,32,4]{5,4,3,2,1,0:T(8,128)} reshape(f32[1,16,64,128]{3,2,1,0:T(8,128)S(1)} %fusion.56) | data formatting | bytes 1048576 | tf_op jit(solution)/shard_map/while/body/eval_jaxpr/add | solution.py:52
  127.0 7.1 %reduce_sum.14 = f32[4,16,32]{2,1,0:T(8,128)S(1)} reduce(f32[4,4,16,4,32,4]{5,4,3,2,1,0:T(8,128)} %add.415, f32[]{:T(128)} %constant.122.clone.1..sunk), dimensions={1,3,5}, to_apply=%region_5.5 | reduce | flops 129024 | bytes 532484 | tf_op jit(solution)/shard_map/while/body/eval_jaxpr/reduce_sum | solution.py:44
  137.5 1.7 fusion.56
  139.2 18.6 %add.415 = f32[4,4,16,4,32,4]{5,4,3,2,1,0:T(8,128)} reshape(f32[1,16,64,128]{3,2,1,0:T(8,128)S(1)} %fusion.56) | data formatting | bytes 1048576 | tf_op jit(solution)/shard_map/while/body/eval_jaxpr/add | solution.py:52
  157.9 7.1 %reduce_sum.14 = f32[4,16,32]{2,1,0:T(8,128)S(1)} reduce(f32[4,4,16,4,32,4]{5,4,3,2,1,0:T(8,128)} %add.415, f32[]{:T(128)} %constant.122.clone.1..sunk), dimensions={1,3,5}, to_apply=%region_5.5 | reduce | flops 129024 | bytes 532484 | tf_op jit(solution)/shard_map/while/body/eval_jaxpr/reduce_sum | solution.py:44
  168.3 1.7 fusion.56
  170.0 18.6 %add.415 = f32[4,4,16,4,32,4]{5,4,3,2,1,0:T(8,128)} reshape(f32[1,16,64,128]{3,2,1,0:T(8,128)S(1)} %fusion.56) | data formatting | bytes 1048576 | tf_op jit(solution)/shard_map/while/body/eval_jaxpr/add | solution.py:52
  188.7 7.1 %reduce_sum.14 = f32[4,16,32]{2,1,0:T(8,128)S(1)} reduce(f32[4,4,16,4,32,4]{5,4,3,2,1,0:T(8,128)} %add.415, f32[]{:T(128)} %constant.122.clone.1..sunk), dimensions={1,3,5}, to_apply=%region_5.5 | reduce | flops 129024 | bytes 532484 | tf_op jit(solution)/shard_map/while/body/eval_jaxpr/reduce_sum | solution.py:44
  199.2 1.7 fusion.56
  200.8 18.6 %add.415 = f32[4,4,16,4,32,4]{5,4,3,2,1,0:T(8,128)} reshape(f32[1,16,64,128]{3,2,1,0:T(8,128)S(1)} %fusion.56) | data formatting | bytes 1048576 | tf_op jit(solution)/shard_map/while/body/eval_jaxpr/add | solution.py:52
  219.5 7.1 %reduce_sum.14 = f32[4,16,32]{2,1,0:T(8,128)S(1)} reduce(f32[4,4,16,4,32,4]{5,4,3,2,1,0:T(8,128)} %add.415, f32[]{:T(128)} %constant.122.clone.1..sunk), dimensions={1,3,5}, to_apply=%region_5.5 | reduce | flops 129024 | bytes 532484 | tf_op jit(solution)/shard_map/while/body/eval_jaxpr/reduce_sum | solution.py:44
  230.0 1.7 fusion.56
  231.7 18.6 %add.415 = f32[4,4,16,4,32,4]{5,4,3,2,1,0:T(8,128)} reshape(f32[1,16,64,128]{3,2,1,0:T(8,128)S(1)} %fusion.56) | data formatting | bytes 1048576 | tf_op jit(solution)/shard_map/while/body/eval_jaxpr/add | solution.py:52
  250.3 7.1 %reduce_sum.14 = f32[4,16,32]{2,1,0:T(8,128)S(1)} reduce(f32[4,4,16,4,32,4]{5,4,3,2,1,0:T(8,128)} %add.415, f32[]{:T(128)} %constant.122.clone.1..sunk), dimensions={1,3,5}, to_apply=%region_5.5 | reduce | flops 129024 | bytes 532484 | tf_op jit(solution)/shard_map/while/body/eval_jaxpr/reduce_sum | solution.py:44
  260.8 1.7 fusion.56
  262.5 18.6 %add.415 = f32[4,4,16,4,32,4]{5,4,3,2,1,0:T(8,128)} reshape(f32[1,16,64,128]{3,2,1,0:T(8,128)S(1)} %fusion.56) | data formatting | bytes 1048576 | tf_op jit(solution)/shard_map/while/body/eval_jaxpr/add | solution.py:52
  281.1 7.1 %reduce_sum.14 = f32[4,16,32]{2,1,0:T(8,128)S(1)} reduce(f32[4,4,16,4,32,4]{5,4,3,2,1,0:T(8,128)} %add.415, f32[]{:T(128)} %constant.122.clone.1..sunk), dimensions={1,3,5}, to_apply=%region_5.5 | reduce | flops 129024 | bytes 532484 | tf_op jit(solution)/shard_map/while/body/eval_jaxpr/reduce_sum | solution.py:44
  291.6 1.7 fusion.56
  293.3 18.6 %add.415 = f32[4,4,16,4,32,4]{5,4,3,2,1,0:T(8,128)} reshape(f32[1,16,64,128]{3,2,1,0:T(8,128)S(1)} %fusion.56) | data formatting | bytes 1048576 | tf_op jit(solution)/shard_map/while/body/eval_jaxpr/add | solution.py:52
  312.0 7.1 %reduce_sum.14 = f32[4,16,32]{2,1,0:T(8,128)S(1)} reduce(f32[4,4,16,4,32,4]{5,4,3,2,1,0:T(8,128)} %add.415, f32[]{:T(128)} %constant.122.clone.1..sunk), dimensions={1,3,5}, to_apply=%region_5.5 | reduce | flops 129024 | bytes 532484 | tf_op jit(solution)/shard_map/while/body/eval_jaxpr/reduce_sum | solution.py:44
  322.4 1.7 fusion.56
  324.1 18.6 %add.415 = f32[4,4,16,4,32,4]{5,4,3,2,1,0:T(8,128)} reshape(f32[1,16,64,128]{3,2,1,0:T(8,128)S(1)} %fusion.56) | data formatting | bytes 1048576 | tf_op jit(solution)/shard_map/while/body/eval_jaxpr/add | solution.py:52
  342.8 7.1 %reduce_sum.14 = f32[4,16,32]{2,1,0:T(8,128)S(1)} reduce(f32[4,4,16,4,32,4]{5,4,3,2,1,0:T(8,128)} %add.415, f32[]{:T(128)} %constant.122.clone.1..sunk), dimensions={1,3,5}, to_apply=%region_5.5 | reduce | flops 129024 | bytes 532484 | tf_op jit(solution)/shard_map/while/body/eval_jaxpr/reduce_sum | solution.py:44
  350.5 123.0 %all-reduce.5.cloned.1.call-done = f32[9,4,16,32]{3,2,1,0:T(8,128)} async-done(((f32[9,4,16,32]{3,2,1,0:T(8,128)}), f32[9,4,16,32]{3,2,1,0:T(8,128)}) %all-reduce.5.cloned.1.call-update) | async-done | bytes 73744 | tf_op jit(solution)/shard_map/psum | solution.py:126
  474.4 15.8 %collective-permute-start.6 = (f32[9,1,16,32]{3,2,1,0:T(8,128)S(1)}, f32[9,1,16,32]{3,2,1,0:T(8,128)S(1)}, u32[]{:S(2)}, u32[]{:S(2)}) collective-permute-start(f32[9,1,16,32]{3,2,1,0:T(8,128)S(1)} %get-tuple-element.88), channel_id=1, source_target_pairs={{0,1},{1,2},{2,3},{3,4},{4,5},{5,6},{6,7},{7,8},{8,9},{9,10},{10,1... | collective-permute-start | bytes 55304 | tf_op jit(solution)/shard_map/ppermute | solution.py:14
  490.2 1.9 collective-permute-start.7
  492.3 7.2 %collective-permute-done.7 = f32[9,1,16,32]{3,2,1,0:T(8,128)S(1)} collective-permute-done((f32[9,1,16,32]{3,2,1,0:T(8,128)S(1)}, f32[9,1,16,32]{3,2,1,0:T(8,128)S(1)}, u32[]{:S(2)}, u32[]{:S(2)}) %collective-permute-start.7) | collective-permute-done | bytes 18464 | tf_op jit(solution)/shard_map/ppermute | solution.py:17
  499.5 1.2 fusion.36
  (83 shorter events, 20.7 us)
Async XLA Ops:
  6.5 19.2 %copy-start = (f32[16,64,128]{2,1,0:T(8,128)S(1)}, f32[16,64,128]{2,1,0:T(8,128)}, u32[]{:S(2)}) copy-start(f32[16,64,128]{2,1,0:T(8,128)} %param.18) | copy-start | bytes 1572868
  6.5 466.9 %all-reduce.5.cloned.1.call-start = ((), (), s32[]{:S(2)}) async-start(), calls=%async_computation | async-start | bytes 589824 | tf_op jit(solution)/shard_map/psum | solution.py:126
  8.8 17.0 %collective-permute-start = (f32[2,1,64,128]{3,2,1,0:T(8,128)S(1)}, f32[2,1,64,128]{3,2,1,0:T(8,128)S(1)}, u32[]{:S(2)}, u32[]{:S(2)}) collective-permute-start(f32[2,1,64,128]{3,2,1,0:T(8,128)S(1)} %get-tuple-element.85), channel_id=1, source_target_pairs={{1,0},{2,1},{3,2},{4,3},{5,4},{6,5},{7,6},{8,7},{9,8},{10,9},{11,1... | collective-permute-start | bytes 196616 | tf_op jit(solution)/shard_map/ppermute | solution.py:17
  11.4 14.4 %collective-permute-start.1 = (f32[2,1,64,128]{3,2,1,0:T(8,128)S(1)}, f32[2,1,64,128]{3,2,1,0:T(8,128)S(1)}, u32[]{:S(2)}, u32[]{:S(2)}) collective-permute-start(f32[2,1,64,128]{3,2,1,0:T(8,128)S(1)} %get-tuple-element.86), channel_id=1, source_target_pairs={{0,1},{1,2},{2,3},{3,4},{4,5},{5,6},{6,7},{7,8},{8,9},{9,10},{10,1... | collective-permute-start | bytes 196616 | tf_op jit(solution)/shard_map/ppermute | solution.py:14
  27.7 14.8 %collective-permute-start.2 = (f32[2,1,64,128]{3,2,1,0:T(8,128)S(1)}, f32[2,1,64,128]{3,2,1,0:T(8,128)S(1)}, u32[]{:S(2)}, u32[]{:S(2)}) collective-permute-start(f32[2,1,64,128]{3,2,1,0:T(8,128)S(1)} %get-tuple-element.83), channel_id=1, source_target_pairs={{1,0},{2,1},{3,2},{4,3},{5,4},{6,5},{7,6},{8,7},{9,8},{10,9},{11,1... | collective-permute-start | bytes 196616 | tf_op jit(solution)/shard_map/ppermute | solution.py:17
  29.7 12.9 %collective-permute-start.3 = (f32[2,1,64,128]{3,2,1,0:T(8,128)S(1)}, f32[2,1,64,128]{3,2,1,0:T(8,128)S(1)}, u32[]{:S(2)}, u32[]{:S(2)}) collective-permute-start(f32[2,1,64,128]{3,2,1,0:T(8,128)S(1)} %get-tuple-element.84), channel_id=1, source_target_pairs={{0,1},{1,2},{2,3},{3,4},{4,5},{5,6},{6,7},{7,8},{8,9},{9,10},{10,1... | collective-permute-start | bytes 196616 | tf_op jit(solution)/shard_map/ppermute | solution.py:14
  45.7 15.6 %collective-permute-start.4 = (f32[4,8,64,128]{3,2,1,0:T(8,128)}, f32[4,8,64,128]{3,2,1,0:T(8,128)}, u32[]{:S(2)}, u32[]{:S(2)}) collective-permute-start(f32[4,8,64,128]{3,2,1,0:T(8,128)} %get-tuple-element.81), channel_id=1, source_target_pairs={{0,1},{1,2},{2,3},{3,4},{4,5},{5,6},{6,7},{7,8},{8,9},{9,10},{10,1... | collective-permute-start | bytes 3145736 | tf_op jit(solution)/shard_map/ppermute | solution.py:14
  49.2 19.8 %collective-permute-start.5 = (f32[4,8,64,128]{3,2,1,0:T(8,128)S(1)}, f32[4,8,64,128]{3,2,1,0:T(8,128)}, u32[]{:S(2)}, u32[]{:S(2)}) collective-permute-start(f32[4,8,64,128]{3,2,1,0:T(8,128)S(1)} %get-tuple-element.82), channel_id=1, source_target_pairs={{1,0},{2,1},{3,2},{4,3},{5,4},{6,5},{7,6},{8,7},{9,8},{10,9},{11,1... | collective-permute-start | bytes 3145736 | tf_op jit(solution)/shard_map/ppermute | solution.py:17
  51.2 21.9 %copy-start.3 = (s32[9]{0:T(128)S(1)}, s32[9]{0:T(128)}, u32[]{:S(2)}) copy-start(s32[9]{0:T(128)} %param.23) | copy-start | bytes 112
  73.1 419.2 %copy-start.1 = (f32[64,9,3,3,3]{0,4,3,2,1:T(4,128)S(1)}, f32[64,9,3,3,3]{0,4,3,2,1:T(4,128)}, u32[]{:S(2)}) copy-start(f32[64,9,3,3,3]{0,4,3,2,1:T(4,128)} %param.24) | copy-start | bytes 186628
  350.4 151.8 %copy-start.2 = (f32[64]{0:T(128)S(1)}, f32[64]{0:T(128)}, u32[]{:S(2)}) copy-start(f32[64]{0:T(128)} %param.25) | copy-start | bytes 772
  474.4 17.9 %collective-permute-start.6 = (f32[9,1,16,32]{3,2,1,0:T(8,128)S(1)}, f32[9,1,16,32]{3,2,1,0:T(8,128)S(1)}, u32[]{:S(2)}, u32[]{:S(2)}) collective-permute-start(f32[9,1,16,32]{3,2,1,0:T(8,128)S(1)} %get-tuple-element.88), channel_id=1, source_target_pairs={{0,1},{1,2},{2,3},{3,4},{4,5},{5,6},{6,7},{7,8},{8,9},{9,10},{10,1... | collective-permute-start | bytes 55304 | tf_op jit(solution)/shard_map/ppermute | solution.py:14
  490.2 9.3 %collective-permute-start.7 = (f32[9,1,16,32]{3,2,1,0:T(8,128)S(1)}, f32[9,1,16,32]{3,2,1,0:T(8,128)S(1)}, u32[]{:S(2)}, u32[]{:S(2)}) collective-permute-start(f32[9,1,16,32]{3,2,1,0:T(8,128)S(1)} %get-tuple-element.87), channel_id=1, source_target_pairs={{1,0},{2,1},{3,2},{4,3},{5,4},{6,5},{7,6},{8,7},{9,8},{10,9},{11,1... | collective-permute-start | bytes 55304 | tf_op jit(solution)/shard_map/ppermute | solution.py:17
Sparse Core Ops, SparseCore 0:
  350.6 122.8 all-reduce.4
where the time goes:
time: 512 us; the launch traced here: 510 us
  local copies, waits for them, and re-layouts  181 us (35%)
  waiting for transfers between devices  148 us (29%)
  other arithmetic  105 us (21%)
  starting transfers between devices  41.5 us (8%)
  loops' own time  20.3 us (4%)
  between operations  13.8 us (3%)
    add x9, local copies, waits for them, and re-layouts, per_offset(): forward_part[0] * backward_part[1] + forward_part[2] * backward_part[3]  168 us
    psum x1, waiting for transfers between devices, local(): summed = lax.psum(coarse, 'shot')  123 us
    reduce_sum x9, other arithmetic, coarsen(): image_block.reshape(size_x // 4, 4, size_y // 4, 4, size_z // 4, 4)  63.6 us
    ppermute x4, starting transfers between devices, padded_2(): lax.ppermute(lax.slice_in_dim(block, block.shape[dim] - width, None, axis...  33.2 us
    another operation x1, loops' own time, offset_image(): return lax.map(per_offset, offsets)  20.3 us
    add x9, other arithmetic, per_offset(): forward_part[0] * backward_part[1] + forward_part[2] * backward_part[3]  15.1 us
    ppermute x4, waiting for transfers between devices, padded_2(): lax.ppermute(lax.slice_in_dim(block, 0, width, axis=dim), axis, backward)  15 us
  transfers between devices with their start and end apart: 9, of which 4 were waited for; matrix products, arithmetic and copies ran while one was open for 3% of the time, Pallas kernels for 0%

commit v1 on v0

--- a/solution.py
+++ b/solution.py
@@ -123,7 +123,7 @@
     fields = jnp.concatenate(levels, axis=0)
     wide = padded_2(fields, (("gx", 1),), HMAX)
     coarse = offset_image(wide, offsets, HMAX, cells_x)
-    summed = lax.psum(coarse, "shot")
+    summed = jnp.sum(lax.all_gather(coarse, "shot"), axis=0)
     rimmed = padded_2(summed, (("gx", 1),), 1)
     row_count = summed.shape[2] // lax.axis_size("shot")
     padded = jnp.pad(rimmed, ((0, 0), (0, 0), (1, 1), (1, 1)))

time: 512 us -> 456 us (0.89)
  waiting for transfers between devices: 148 us -> 93.2 us
    psum x1 -> x0, waiting for transfers between devices: 123 us -> none  [local(): summed = lax.psum(coarse, 'shot')]
    all_gather x0 -> x1, waiting for transfers between devices: none -> 68.1 us  [local(): summed = jnp.sum(lax.all_gather(coarse, 'shot'), axis=0)]
where the time goes in v1:
time: 456 us; the launch traced here: 455 us
  local copies, waits for them, and re-layouts  180 us (39%)
  other arithmetic  107 us (23%)
  waiting for transfers between devices  93.2 us (20%)
  starting transfers between devices  39.9 us (9%)
  loops' own time  20.3 us (4%)
  between operations  13.8 us (3%)
    add x9, local copies, waits for them, and re-layouts, per_offset(): forward_part[0] * backward_part[1] + forward_part[2] * backward_part[3]  168 us
    all_gather x1, waiting for transfers between devices, local(): summed = jnp.sum(lax.all_gather(coarse, 'shot'), axis=0)  68.1 us
    reduce_sum x9, other arithmetic, coarsen(): image_block.reshape(size_x // 4, 4, size_y // 4, 4, size_z // 4, 4)  63.6 us
    ppermute x4, starting transfers between devices, padded_2(): lax.ppermute(lax.slice_in_dim(block, block.shape[dim] - width, None, axis...  31.6 us
    another operation x1, loops' own time, offset_image(): return lax.map(per_offset, offsets)  20.3 us
    add x9, other arithmetic, per_offset(): forward_part[0] * backward_part[1] + forward_part[2] * backward_part[3]  15.1 us
    ppermute x4, waiting for transfers between devices, padded_2(): lax.ppermute(lax.slice_in_dim(block, 0, width, axis=dim), axis, backward)  15 us
    ppermute x4, waiting for transfers between devices, padded_2(): lax.ppermute(lax.slice_in_dim(block, block.shape[dim] - width, None, axis...  10.1 us
  transfers between devices with their start and end apart: 9, of which 4 were waited for; matrix products, arithmetic and copies ran while one was open for 3% of the time, Pallas kernels for 0%

profile of v1, /device:TPU:7, one launch (start us, length us, event | category | flops | bytes accessed | tf_op | source)
XLA Modules:
  0.0 454.8 jit_solution(6510357783216687768)
XLA Ops:
  6.5 1.1 constant_dynamic-update-slice_fusion.1
  8.8 2.6 collective-permute-start
  11.4 6.6 %collective-permute-start.1 = (f32[2,1,64,128]{3,2,1,0:T(8,128)S(1)}, f32[2,1,64,128]{3,2,1,0:T(8,128)S(1)}, u32[]{:S(2)}, u32[]{:S(2)}) collective-permute-start(f32[2,1,64,128]{3,2,1,0:T(8,128)S(1)} %get-tuple-element.86), channel_id=1, source_target_pairs={{0,1},{1,2},{2,3},{3,4},{4,5},{5,6},{6,7},{7,8},{8,9},{9,10},{10,1... | collective-permute-start | bytes 196616 | tf_op jit(solution)/shard_map/ppermute | solution.py:14
  20.9 4.0 scatter_custom_fusion.1
  25.8 1.9 fusion.10
  27.7 1.9 collective-permute-start.2
  29.7 7.3 %collective-permute-start.3 = (f32[2,1,64,128]{3,2,1,0:T(8,128)S(1)}, f32[2,1,64,128]{3,2,1,0:T(8,128)S(1)}, u32[]{:S(2)}, u32[]{:S(2)}) collective-permute-start(f32[2,1,64,128]{3,2,1,0:T(8,128)S(1)} %get-tuple-element.84), channel_id=1, source_target_pairs={{0,1},{1,2},{2,3},{3,4},{4,5},{5,6},{6,7},{7,8},{8,9},{9,10},{10,1... | collective-permute-start | bytes 196616 | tf_op jit(solution)/shard_map/ppermute | solution.py:14
  36.9 4.0 scatter_custom_fusion.3
  42.6 1.9 fusion.18
  44.5 1.2 fusion.2
  45.7 3.5 collective-permute-start.4
  49.2 1.9 collective-permute-start.5
  51.2 10.1 %collective-permute-done.4 = f32[4,8,64,128]{3,2,1,0:T(8,128)} collective-permute-done((f32[4,8,64,128]{3,2,1,0:T(8,128)}, f32[4,8,64,128]{3,2,1,0:T(8,128)}, u32[]{:S(2)}, u32[]{:S(2)}) %collective-permute-start.4) | collective-permute-done | bytes 1048608 | tf_op jit(solution)/shard_map/ppermute | solution.py:14
  61.3 7.8 %collective-permute-done.5 = f32[4,8,64,128]{3,2,1,0:T(8,128)} collective-permute-done((f32[4,8,64,128]{3,2,1,0:T(8,128)S(1)}, f32[4,8,64,128]{3,2,1,0:T(8,128)}, u32[]{:S(2)}, u32[]{:S(2)}) %collective-permute-start.5) | collective-permute-done | bytes 1048608 | tf_op jit(solution)/shard_map/ppermute | solution.py:17
  69.1 4.0 pad_maximum_fusion
  73.1 277.4 %while.13 = (s32[]{:T(128)}, f32[9,4,16,32]{3,2,1,0:T(8,128)}, s32[9]{0:T(128)S(1)}, f32[4,32,64,128]{3,2,1,0:T(8,128)}, s32[]{:T(128)}, /*index=5*/s32[]{:T(128...) while((s32[]{:T(128)}, f32[9,4,16,32]{3,2,1,0:T(8,128)}, s32[9]{0:T(128)S(1)}, ...), condition=%wide.region_6.7_spmd, body=%wide.region_4.6_spmd.sunk | while | flops 524301 | bytes 4244249 | solution.py:55
  75.9 1.7 fusion.56
  77.6 18.6 %add.413 = f32[4,4,16,4,32,4]{5,4,3,2,1,0:T(8,128)} reshape(f32[1,16,64,128]{3,2,1,0:T(8,128)S(1)} %fusion.56) | data formatting | bytes 1048576 | tf_op jit(solution)/shard_map/while/body/eval_jaxpr/add | solution.py:52
  96.2 7.1 %reduce_sum.24 = f32[4,16,32]{2,1,0:T(8,128)S(1)} reduce(f32[4,4,16,4,32,4]{5,4,3,2,1,0:T(8,128)} %add.413, f32[]{:T(128)} %constant.123.clone.1..sunk), dimensions={1,3,5}, to_apply=%region_5.5 | reduce | flops 129024 | bytes 532484 | tf_op jit(solution)/shard_map/while/body/eval_jaxpr/reduce_sum | solution.py:44
  106.7 1.7 fusion.56
  108.4 18.6 %add.413 = f32[4,4,16,4,32,4]{5,4,3,2,1,0:T(8,128)} reshape(f32[1,16,64,128]{3,2,1,0:T(8,128)S(1)} %fusion.56) | data formatting | bytes 1048576 | tf_op jit(solution)/shard_map/while/body/eval_jaxpr/add | solution.py:52
  127.0 7.1 %reduce_sum.24 = f32[4,16,32]{2,1,0:T(8,128)S(1)} reduce(f32[4,4,16,4,32,4]{5,4,3,2,1,0:T(8,128)} %add.413, f32[]{:T(128)} %constant.123.clone.1..sunk), dimensions={1,3,5}, to_apply=%region_5.5 | reduce | flops 129024 | bytes 532484 | tf_op jit(solution)/shard_map/while/body/eval_jaxpr/reduce_sum | solution.py:44
  137.5 1.7 fusion.56
  139.2 18.6 %add.413 = f32[4,4,16,4,32,4]{5,4,3,2,1,0:T(8,128)} reshape(f32[1,16,64,128]{3,2,1,0:T(8,128)S(1)} %fusion.56) | data formatting | bytes 1048576 | tf_op jit(solution)/shard_map/while/body/eval_jaxpr/add | solution.py:52
  157.9 7.1 %reduce_sum.24 = f32[4,16,32]{2,1,0:T(8,128)S(1)} reduce(f32[4,4,16,4,32,4]{5,4,3,2,1,0:T(8,128)} %add.413, f32[]{:T(128)} %constant.123.clone.1..sunk), dimensions={1,3,5}, to_apply=%region_5.5 | reduce | flops 129024 | bytes 532484 | tf_op jit(solution)/shard_map/while/body/eval_jaxpr/reduce_sum | solution.py:44
  168.3 1.7 fusion.56
  170.0 18.6 %add.413 = f32[4,4,16,4,32,4]{5,4,3,2,1,0:T(8,128)} reshape(f32[1,16,64,128]{3,2,1,0:T(8,128)S(1)} %fusion.56) | data formatting | bytes 1048576 | tf_op jit(solution)/shard_map/while/body/eval_jaxpr/add | solution.py:52
  188.7 7.1 %reduce_sum.24 = f32[4,16,32]{2,1,0:T(8,128)S(1)} reduce(f32[4,4,16,4,32,4]{5,4,3,2,1,0:T(8,128)} %add.413, f32[]{:T(128)} %constant.123.clone.1..sunk), dimensions={1,3,5}, to_apply=%region_5.5 | reduce | flops 129024 | bytes 532484 | tf_op jit(solution)/shard_map/while/body/eval_jaxpr/reduce_sum | solution.py:44
  199.2 1.7 fusion.56
  200.8 18.6 %add.413 = f32[4,4,16,4,32,4]{5,4,3,2,1,0:T(8,128)} reshape(f32[1,16,64,128]{3,2,1,0:T(8,128)S(1)} %fusion.56) | data formatting | bytes 1048576 | tf_op jit(solution)/shard_map/while/body/eval_jaxpr/add | solution.py:52
  219.5 7.1 %reduce_sum.24 = f32[4,16,32]{2,1,0:T(8,128)S(1)} reduce(f32[4,4,16,4,32,4]{5,4,3,2,1,0:T(8,128)} %add.413, f32[]{:T(128)} %constant.123.clone.1..sunk), dimensions={1,3,5}, to_apply=%region_5.5 | reduce | flops 129024 | bytes 532484 | tf_op jit(solution)/shard_map/while/body/eval_jaxpr/reduce_sum | solution.py:44
  230.0 1.7 fusion.56
  231.7 18.6 %add.413 = f32[4,4,16,4,32,4]{5,4,3,2,1,0:T(8,128)} reshape(f32[1,16,64,128]{3,2,1,0:T(8,128)S(1)} %fusion.56) | data formatting | bytes 1048576 | tf_op jit(solution)/shard_map/while/body/eval_jaxpr/add | solution.py:52
  250.3 7.1 %reduce_sum.24 = f32[4,16,32]{2,1,0:T(8,128)S(1)} reduce(f32[4,4,16,4,32,4]{5,4,3,2,1,0:T(8,128)} %add.413, f32[]{:T(128)} %constant.123.clone.1..sunk), dimensions={1,3,5}, to_apply=%region_5.5 | reduce | flops 129024 | bytes 532484 | tf_op jit(solution)/shard_map/while/body/eval_jaxpr/reduce_sum | solution.py:44
  260.8 1.7 fusion.56
  262.5 18.6 %add.413 = f32[4,4,16,4,32,4]{5,4,3,2,1,0:T(8,128)} reshape(f32[1,16,64,128]{3,2,1,0:T(8,128)S(1)} %fusion.56) | data formatting | bytes 1048576 | tf_op jit(solution)/shard_map/while/body/eval_jaxpr/add | solution.py:52
  281.1 7.1 %reduce_sum.24 = f32[4,16,32]{2,1,0:T(8,128)S(1)} reduce(f32[4,4,16,4,32,4]{5,4,3,2,1,0:T(8,128)} %add.413, f32[]{:T(128)} %constant.123.clone.1..sunk), dimensions={1,3,5}, to_apply=%region_5.5 | reduce | flops 129024 | bytes 532484 | tf_op jit(solution)/shard_map/while/body/eval_jaxpr/reduce_sum | solution.py:44
  291.6 1.7 fusion.56
  293.3 18.6 %add.413 = f32[4,4,16,4,32,4]{5,4,3,2,1,0:T(8,128)} reshape(f32[1,16,64,128]{3,2,1,0:T(8,128)S(1)} %fusion.56) | data formatting | bytes 1048576 | tf_op jit(solution)/shard_map/while/body/eval_jaxpr/add | solution.py:52
  311.9 7.1 %reduce_sum.24 = f32[4,16,32]{2,1,0:T(8,128)S(1)} reduce(f32[4,4,16,4,32,4]{5,4,3,2,1,0:T(8,128)} %add.413, f32[]{:T(128)} %constant.123.clone.1..sunk), dimensions={1,3,5}, to_apply=%region_5.5 | reduce | flops 129024 | bytes 532484 | tf_op jit(solution)/shard_map/while/body/eval_jaxpr/reduce_sum | solution.py:44
  322.4 1.7 fusion.56
  324.1 18.6 %add.413 = f32[4,4,16,4,32,4]{5,4,3,2,1,0:T(8,128)} reshape(f32[1,16,64,128]{3,2,1,0:T(8,128)S(1)} %fusion.56) | data formatting | bytes 1048576 | tf_op jit(solution)/shard_map/while/body/eval_jaxpr/add | solution.py:52
  342.8 7.1 %reduce_sum.24 = f32[4,16,32]{2,1,0:T(8,128)S(1)} reduce(f32[4,4,16,4,32,4]{5,4,3,2,1,0:T(8,128)} %add.413, f32[]{:T(128)} %constant.123.clone.1..sunk), dimensions={1,3,5}, to_apply=%region_5.5 | reduce | flops 129024 | bytes 532484 | tf_op jit(solution)/shard_map/while/body/eval_jaxpr/reduce_sum | solution.py:44
  350.5 68.1 %all-gather.3.cloned.1.call-done = f32[144,4,16,32]{3,2,1,0:T(8,128)} async-done(((f32[9,4,16,32]{3,2,1,0:T(8,128)}), f32[144,4,16,32]{3,2,1,0:T(8,128)}) %all-gather.3.cloned.1.call-update) | async-done | bytes 1179664 | tf_op jit(solution)/shard_map/all_gather | solution.py:126
  418.6 2.9 reduce_sum.22
  421.5 14.2 %collective-permute-start.6 = (f32[9,1,16,32]{3,2,1,0:T(8,128)S(1)}, f32[9,1,16,32]{3,2,1,0:T(8,128)S(1)}, u32[]{:S(2)}, u32[]{:S(2)}) collective-permute-start(f32[9,1,16,32]{3,2,1,0:T(8,128)S(1)} %get-tuple-element.88), channel_id=1, source_target_pairs={{0,1},{1,2},{2,3},{3,4},{4,5},{5,6},{6,7},{7,8},{8,9},{9,10},{10,1... | collective-permute-start | bytes 55304 | tf_op jit(solution)/shard_map/ppermute | solution.py:14
  435.7 1.9 collective-permute-start.7
  437.8 7.2 %collective-permute-done.7 = f32[9,1,16,32]{3,2,1,0:T(8,128)S(1)} collective-permute-done((f32[9,1,16,32]{3,2,1,0:T(8,128)S(1)}, f32[9,1,16,32]{3,2,1,0:T(8,128)S(1)}, u32[]{:S(2)}, u32[]{:S(2)}) %collective-permute-start.7) | collective-permute-done | bytes 18464 | tf_op jit(solution)/shard_map/ppermute | solution.py:17
  (84 shorter events, 20.0 us)
Async XLA Ops:
  6.5 19.2 %copy-start = (f32[16,64,128]{2,1,0:T(8,128)S(1)}, f32[16,64,128]{2,1,0:T(8,128)}, u32[]{:S(2)}) copy-start(f32[16,64,128]{2,1,0:T(8,128)} %param.18) | copy-start | bytes 1572868
  6.5 412.0 %all-gather.3.cloned.1.call-start = ((), (), s32[]{:S(2)}) async-start(), calls=%async_computation | async-start | bytes 5013504 | tf_op jit(solution)/shard_map/all_gather | solution.py:126
  8.8 17.0 %collective-permute-start = (f32[2,1,64,128]{3,2,1,0:T(8,128)S(1)}, f32[2,1,64,128]{3,2,1,0:T(8,128)S(1)}, u32[]{:S(2)}, u32[]{:S(2)}) collective-permute-start(f32[2,1,64,128]{3,2,1,0:T(8,128)S(1)} %get-tuple-element.85), channel_id=1, source_target_pairs={{1,0},{2,1},{3,2},{4,3},{5,4},{6,5},{7,6},{8,7},{9,8},{10,9},{11,1... | collective-permute-start | bytes 196616 | tf_op jit(solution)/shard_map/ppermute | solution.py:17
  11.4 14.4 %collective-permute-start.1 = (f32[2,1,64,128]{3,2,1,0:T(8,128)S(1)}, f32[2,1,64,128]{3,2,1,0:T(8,128)S(1)}, u32[]{:S(2)}, u32[]{:S(2)}) collective-permute-start(f32[2,1,64,128]{3,2,1,0:T(8,128)S(1)} %get-tuple-element.86), channel_id=1, source_target_pairs={{0,1},{1,2},{2,3},{3,4},{4,5},{5,6},{6,7},{7,8},{8,9},{9,10},{10,1... | collective-permute-start | bytes 196616 | tf_op jit(solution)/shard_map/ppermute | solution.py:14
  27.7 14.8 %collective-permute-start.2 = (f32[2,1,64,128]{3,2,1,0:T(8,128)S(1)}, f32[2,1,64,128]{3,2,1,0:T(8,128)S(1)}, u32[]{:S(2)}, u32[]{:S(2)}) collective-permute-start(f32[2,1,64,128]{3,2,1,0:T(8,128)S(1)} %get-tuple-element.83), channel_id=1, source_target_pairs={{1,0},{2,1},{3,2},{4,3},{5,4},{6,5},{7,6},{8,7},{9,8},{10,9},{11,1... | collective-permute-start | bytes 196616 | tf_op jit(solution)/shard_map/ppermute | solution.py:17
  29.7 12.9 %collective-permute-start.3 = (f32[2,1,64,128]{3,2,1,0:T(8,128)S(1)}, f32[2,1,64,128]{3,2,1,0:T(8,128)S(1)}, u32[]{:S(2)}, u32[]{:S(2)}) collective-permute-start(f32[2,1,64,128]{3,2,1,0:T(8,128)S(1)} %get-tuple-element.84), channel_id=1, source_target_pairs={{0,1},{1,2},{2,3},{3,4},{4,5},{5,6},{6,7},{7,8},{8,9},{9,10},{10,1... | collective-permute-start | bytes 196616 | tf_op jit(solution)/shard_map/ppermute | solution.py:14
  45.7 15.6 %collective-permute-start.4 = (f32[4,8,64,128]{3,2,1,0:T(8,128)}, f32[4,8,64,128]{3,2,1,0:T(8,128)}, u32[]{:S(2)}, u32[]{:S(2)}) collective-permute-start(f32[4,8,64,128]{3,2,1,0:T(8,128)} %get-tuple-element.81), channel_id=1, source_target_pairs={{0,1},{1,2},{2,3},{3,4},{4,5},{5,6},{6,7},{7,8},{8,9},{9,10},{10,1... | collective-permute-start | bytes 3145736 | tf_op jit(solution)/shard_map/ppermute | solution.py:14
  49.2 19.8 %collective-permute-start.5 = (f32[4,8,64,128]{3,2,1,0:T(8,128)S(1)}, f32[4,8,64,128]{3,2,1,0:T(8,128)}, u32[]{:S(2)}, u32[]{:S(2)}) collective-permute-start(f32[4,8,64,128]{3,2,1,0:T(8,128)S(1)} %get-tuple-element.82), channel_id=1, source_target_pairs={{1,0},{2,1},{3,2},{4,3},{5,4},{6,5},{7,6},{8,7},{9,8},{10,9},{11,1... | collective-permute-start | bytes 3145736 | tf_op jit(solution)/shard_map/ppermute | solution.py:17
  51.2 21.9 %copy-start.3 = (s32[9]{0:T(128)S(1)}, s32[9]{0:T(128)}, u32[]{:S(2)}) copy-start(s32[9]{0:T(128)} %param.23) | copy-start | bytes 112
  350.4 87.3 %copy-start.1 = (f32[64,9,3,3,3]{0,4,3,2,1:T(4,128)S(1)}, f32[64,9,3,3,3]{0,4,3,2,1:T(4,128)}, u32[]{:S(2)}) copy-start(f32[64,9,3,3,3]{0,4,3,2,1:T(4,128)} %param.24) | copy-start | bytes 186628
  418.6 28.3 %copy-start.2 = (f32[64]{0:T(128)S(1)}, f32[64]{0:T(128)}, u32[]{:S(2)}) copy-start(f32[64]{0:T(128)} %param.25) | copy-start | bytes 772
  421.5 16.3 %collective-permute-start.6 = (f32[9,1,16,32]{3,2,1,0:T(8,128)S(1)}, f32[9,1,16,32]{3,2,1,0:T(8,128)S(1)}, u32[]{:S(2)}, u32[]{:S(2)}) collective-permute-start(f32[9,1,16,32]{3,2,1,0:T(8,128)S(1)} %get-tuple-element.88), channel_id=1, source_target_pairs={{0,1},{1,2},{2,3},{3,4},{4,5},{5,6},{6,7},{7,8},{8,9},{9,10},{10,1... | collective-permute-start | bytes 55304 | tf_op jit(solution)/shard_map/ppermute | solution.py:14
  435.7 9.3 %collective-permute-start.7 = (f32[9,1,16,32]{3,2,1,0:T(8,128)S(1)}, f32[9,1,16,32]{3,2,1,0:T(8,128)S(1)}, u32[]{:S(2)}, u32[]{:S(2)}) collective-permute-start(f32[9,1,16,32]{3,2,1,0:T(8,128)S(1)} %get-tuple-element.87), channel_id=1, source_target_pairs={{1,0},{2,1},{3,2},{4,3},{5,4},{6,5},{7,6},{8,7},{9,8},{10,9},{11,1... | collective-permute-start | bytes 55304 | tf_op jit(solution)/shard_map/ppermute | solution.py:17
Sparse Core Ops, SparseCore 0:
  350.6 67.9 all-gather.2
